TPU v7x, 32 devices: a whole 2x2x4 slice. The times are simulated.
32 devices in a mesh: groups: 2 (over y), corr: 4 (over z), filt: 2 (over x), pair: 2 (over core).
Axes of the slice: x: 2, y: 2, z: 4, core: 2. Of those that a mesh axis runs over, the one named last changes fastest.
Arguments:
- raw_rows: bfloat16 [4, 32, 3, 16384], P(('groups', 'pair'), 'filt', None, 'corr'), parts along dimension 0, may hold values from -6 to 6
- valid_counts: int32 [4, 32], P(('groups', 'pair'), 'filt'), parts along dimension 0, may hold values from 4096 to 16384
- taps: bfloat16 [64], replicated, may hold values from -0.75 to 0.75
- templates: bfloat16 [128, 225], P('corr'), may hold values from -6 to 6
- masks: int32 [128, 3, 32], replicated, may hold values 0 or 1
Outputs:
- stack: float32 [4, 128, 4096], P(('groups', 'pair'), 'corr', 'filt'), parts along dimension 0
There are 2 independent parts, one for each index of `groups`. A program takes and returns all parts, laid end to end along the dimension named above; an argument that names none is the same for every part. Nothing has to cross between parts.
All inputs are finite; a program needn't handle non-finite values.
Results may differ from a plain program's by a relative error of at most 0.0051.
Values may be sent and summed in bfloat16 or wider, within the bound.
No kernel may reach another device: no remote copies, remote signals or barrier semaphores. Data moves between devices by JAX's collectives and lax.ppermute only.
A program may use at most 192 MiB of HBM per device.

v0:
```python
import jax
import jax.numpy as jnp
from jax import lax
from jax.sharding import PartitionSpec as P

L = 75
TAPS = 64
DEC = 4


def from_behind(block, axis, distance):
    devices = range(lax.axis_size(axis))
    route = [(i - distance, i) for i in devices if i - distance in devices]
    return lax.ppermute(block, axis, route)


def scaled_rows(extended):
    station_count = extended.shape[0]
    width = extended.shape[2] - (L - 1)
    slices = jnp.stack([extended[:, :, lag : lag + width] for lag in range(L)], axis=2)
    energy = jnp.einsum("scjt,scjt->sct", slices, slices, preferred_element_type=jnp.float32)
    scaled = (slices / jnp.sqrt(jnp.maximum(energy, 1.0))[:, :, None, :]).astype(jnp.bfloat16)
    return scaled.reshape(station_count * 3 * L, width)


def template_weights(template_rows, mask_rows):
    count = template_rows.shape[0]
    stations = mask_rows.shape[2]
    shaped = template_rows.astype(jnp.float32).reshape(count, 3, L)
    norms = jnp.sqrt(jnp.sum(shaped * shaped, axis=2) + 1e-06)
    base = shaped / norms[:, :, None]
    chosen = jnp.transpose(mask_rows.astype(jnp.float32), (0, 2, 1))
    full = base[:, None, :, :] * chosen[:, :, :, None]
    return full.astype(jnp.bfloat16).reshape(count, stations * 3 * L)


def body(raw_rows, valid_counts, taps, templates, masks):
    samples = raw_rows[0]
    counts = valid_counts[0]
    local_stations = samples.shape[0]
    raw_width = samples.shape[2]
    corr_place = lax.axis_index("corr")
    corr_count = lax.axis_size("corr")
    filt_count = lax.axis_size("filt")
    template_all = masks.shape[0]
    group_size = masks.shape[2] // (corr_count * filt_count)
    sample_times = corr_place * raw_width + lax.iota(jnp.int32, raw_width)
    live = jnp.where(
        sample_times[None, None, :] < counts[:, None, None], samples, jnp.zeros_like(samples)
    )
    history = from_behind(live[:, :, raw_width - (TAPS - 1) :], "corr", 1)
    extended = jnp.concatenate([history, live], axis=2).reshape(
        local_stations * 3, 1, raw_width + TAPS - 1
    )
    kernel = taps[::-1].reshape(1, 1, TAPS)
    filtered = lax.conv_general_dilated(
        extended,
        kernel,
        (DEC,),
        "VALID",
        dimension_numbers=("NCH", "OIH", "NCH"),
        preferred_element_type=jnp.float32,
    )
    decimated = raw_width // DEC
    filtered = filtered.astype(jnp.bfloat16).reshape(local_stations, 3, decimated)
    moved = lax.all_to_all(
        lax.all_to_all(filtered, "corr", split_axis=0, concat_axis=2, tiled=True),
        "filt",
        split_axis=2,
        concat_axis=0,
        tiled=True,
    )
    following = from_behind(moved[:, :, : L - 1], "filt", -1)
    lagged = jnp.concatenate([moved, following], axis=2)
    block_width = moved.shape[2]
    split_masks = masks.reshape(template_all, 3, filt_count, corr_count, group_size)
    mine = lax.dynamic_slice_in_dim(split_masks, corr_place, 1, 3).reshape(
        template_all, 3, filt_count * group_size
    )
    scaled = scaled_rows(lagged)
    empty = jnp.zeros((template_all, block_width), jnp.float32)
    weights = template_weights(lax.all_gather(templates, "corr", axis=0, tiled=True), mine)
    partial_rows = jnp.dot(weights, scaled, preferred_element_type=jnp.float32)
    totals = lax.dynamic_update_slice_in_dim(empty, partial_rows, jnp.int32(0), 0)
    stacked = lax.psum_scatter(totals, "corr", scatter_dimension=0, tiled=True)
    return stacked[None]


def solution(mesh):
    return jax.shard_map(
        body,
        mesh=mesh,
        in_specs=(
            P(("groups", "pair"), "filt", None, "corr"),
            P(("groups", "pair"), "filt"),
            P(),
            P("corr", None),
            P(),
        ),
        out_specs=P(("groups", "pair"), "corr", "filt"),
        check_vma=False,
    )
```

profile of v0, /device:TPU:0, one launch (start us, length us, event | category | flops | bytes accessed | tf_op | source)
XLA Modules:
  0.0 146.4 jit_solution(11278841921117078168)
XLA Ops:
  6.5 0.8 broadcast_compare_fusion
  7.3 1.0 bitcast_select_fusion
  8.4 4.9 %collective-permute-start = (bf16[16,3,63]{2,0,1:T(8,128)(2,1)S(1)}, bf16[16,3,63]{2,0,1:T(8,128)(2,1)S(1)}, u32[]{:S(2)}, u32[]{:S(2)}) collective-permute-start(bf16[16,3,63]{2,0,1:T(8,128)(2,1)S(1)} %slice.304), channel_id=1, source_target_pairs={{0,4},{4,8},{8,12},{1,5},{5,9},{9,13},{2,6},{6,10},{10,14},{3,7},{... | collective-permute-start | bytes 18152 | tf_op jit(solution)/shard_map/ppermute | solution.py:14
  13.4 13.7 %all_gather.3 = bf16[128,225]{1,0:T(8,128)(2,1)S(1)} all-gather(bf16[32,225]{1,0:T(8,128)(2,1)} %param.8), channel_id=1, replica_groups=mesh['groups'=2,'corr'=4,'filt'=2,'pair'=2] {'corr'}, dimensions={0}, use_global_device_ids=true | all-gather | bytes 72000 | tf_op jit(solution)/shard_map/all_gather | solution.py:82
  27.1 0.1 copy.130
  27.3 0.7 rev.3
  28.0 0.1 copy.134
  28.1 0.2 pad_maximum_fusion
  28.3 0.2 copy.132
  28.5 0.3 reshape.73
  28.9 2.8 %copy.133 = bf16[48,1,4159]{0,1,2:T(2,128)(2,1)S(1)} copy(bf16[48,1,4159]{2,0,1:T(8,128)(2,1)S(1)} %reshape.73) | data formatting | bytes 798528 | tf_op jit(solution)/shard_map/reshape | solution.py:52
  31.7 11.7 %convolution_convert_fusion = bf16[48,1,1024]{0,1,2:T(2,128)(2,1)S(1)} fusion(bf16[48,1,4159]{0,1,2:T(2,128)(2,1)S(1)} %copy.133, bf16[1,1,64]{1,0,2:T(2,128)(2,1)S(1)} %copy.134), kind=kOutput, calls=%fused_computation.6 | convolution fusion | flops 6340608 | bytes 497696 | tf_op jit(solution)/shard_map/conv_general_dilated | solution.py:56
  43.4 0.3 copy.135
  43.7 0.7 reshape.75
  44.5 3.3 %all-to-all-start = ((bf16[16,3,1024]{2,1,0:T(4,128)(2,1)}), bf16[16,3,1024]{2,1,0:T(4,128)(2,1)S(1)}, u32[]{:S(2)}, u32[]{:S(2)}) async-start(bf16[16,3,1024]{2,1,0:T(4,128)(2,1)} %reshape.75), calls=%async_computation | async-start | bytes 262144 | tf_op jit(solution)/shard_map/all_to_all | solution.py:67
  47.8 5.9 %all-to-all-done = bf16[16,3,1024]{2,1,0:T(4,128)(2,1)S(1)} async-done(((bf16[16,3,1024]{2,1,0:T(4,128)(2,1)}), bf16[16,3,1024]{2,1,0:T(4,128)(2,1)S(1)}, u32[]{:S(2)}, u32[]{:S(2)}) %all-to-all-start) | async-done | bytes 98336 | tf_op jit(solution)/shard_map/all_to_all | solution.py:67
  53.7 4.7 %copy.149 = bf16[4,3,4,1024]{0,1,3,2:T(4,128)(2,1)} copy(bf16[4,3,4,1024]{3,1,0,2:T(4,128)(2,1)S(1)} %bitcast.336) | data formatting | bytes 196608 | tf_op jit(solution)/shard_map/all_to_all | solution.py:67
  58.4 5.8 %reshape.81 = bf16[2,2,12288]{2,1,0:T(2,128)(2,1)} reshape(bf16[4096,3,4]{2,1,0:T(4,128)(2,1)} %bitcast.334) | data formatting | bytes 196608
  64.3 3.3 %all-to-all-start.1 = ((bf16[2,2,12288]{2,1,0:T(2,128)(2,1)}), bf16[2,2,12288]{2,1,0:T(2,128)(2,1)S(1)}, u32[]{:S(2)}, u32[]{:S(2)}) async-start(bf16[2,2,12288]{2,1,0:T(2,128)(2,1)} %reshape.81), calls=%async_computation.1 | async-start | bytes 196608 | tf_op jit(solution)/shard_map/all_to_all | solution.py:66
  67.7 0.7 dynamic-slice_convert_fusion
  68.4 3.5 %all-to-all-done.1 = bf16[2,2,12288]{2,1,0:T(2,128)(2,1)S(1)} async-done(((bf16[2,2,12288]{2,1,0:T(2,128)(2,1)}), bf16[2,2,12288]{2,1,0:T(2,128)(2,1)S(1)}, u32[]{:S(2)}, u32[]{:S(2)}) %all-to-all-start.1) | async-done | bytes 98336 | tf_op jit(solution)/shard_map/all_to_all | solution.py:66
  71.9 5.1 %reshape.82 = bf16[4096,3,4]{2,1,0:T(4,128)(2,1)} reshape(bf16[2,2,12288]{2,1,0:T(2,128)(2,1)S(1)} %all-to-all-done.1) | data formatting | bytes 196608
  77.0 5.9 %copy.150 = bf16[4,3,2,2048]{3,2,0,1:T(2,128)(2,1)S(1)} copy(bf16[4,3,2,2048]{0,1,3,2:T(4,128)(2,1)} %bitcast.335) | data formatting | bytes 196608 | tf_op jit(solution)/shard_map/all_to_all | solution.py:66
  83.0 1.5 %collective-permute-start.1 = (bf16[8,3,74]{2,0,1:T(8,128)(2,1)S(1)}, bf16[8,3,74]{2,0,1:T(8,128)(2,1)S(1)}, u32[]{:S(2)}, u32[]{:S(2)}) collective-permute-start(bf16[8,3,74]{2,0,1:T(8,128)(2,1)S(1)} %slice.305), channel_id=1, source_target_pairs={{2,0},{3,1},{6,4},{7,5},{10,8},{11,9},{14,12},{15,13},{18,16},{19,... | collective-permute-start | bytes 10664 | tf_op jit(solution)/shard_map/ppermute | solution.py:14
  84.5 4.0 %collective-permute-done.1 = bf16[8,3,74]{2,0,1:T(8,128)(2,1)S(1)} collective-permute-done((bf16[8,3,74]{2,0,1:T(8,128)(2,1)S(1)}, bf16[8,3,74]{2,0,1:T(8,128)(2,1)S(1)}, u32[]{:S(2)}, u32[]{:S(2)}) %collective-permute-start.1) | collective-permute-done | bytes 3584 | tf_op jit(solution)/shard_map/ppermute | solution.py:14
  88.5 0.1 constant_dynamic-update-slice_fusion.75
  88.6 0.1 constant_dynamic-update-slice_fusion.74
  96.0 1.6 %fusion = f32[8,3,2048]{2,0,1:T(8,128)S(1)} fusion(bf16[8,3,75,2048]{3,0,1,2:T(8,128)(2,1)S(1)} %constant_dynamic-update-slice_fusion.2), kind=kLoop, calls=%fused_computation.1 | loop fusion | flops 11010048 | bytes 7569408 | tf_op jit(solution)/shard_map/scjt,scjt->sct/dot_general | solution.py:21
  97.6 1.4 copy-done
  99.0 5.3 %divide_convert_fusion = bf16[8,3,75,2048]{3,0,1,2:T(8,128)(2,1)S(1)} fusion(bf16[8,3,75,2048]{3,0,1,2:T(8,128)(2,1)} %copy-done, f32[8,3,2048]{2,0,1:T(8,128)S(1)} %maximum_sqrt_fusion), kind=kLoop, calls=%fused_computation.2 | loop fusion | flops 11059200 | bytes 14942208 | tf_op jit(solution)/shard_map/convert_element_type | solution.py:22
  104.3 9.6 %fusion.3 = f32[128,2048]{1,0:T(8,128)} fusion(bf16[8,3,75,2048]{3,0,1,2:T(8,128)(2,1)S(1)} %divide_convert_fusion, f32[128,8,3]{0,2,1:T(4,128)S(1)} %bitcast.338, f32[128,3,75]{0,2,1:T(8,128)S(1)} %broadcast_divide_fusion), kind=kOutput, calls=%fused_computation.5 | convolution fusion | flops 944179200 | bytes 8548864 | tf_op jit(solution)/shard_map/dot_general | solution.py:83
  113.9 25.6 %reduce-scatter.2.cloned.1.call-done = f32[32,2048]{1,0:T(8,128)} async-done(((f32[128,2048]{1,0:T(8,128)}), f32[32,2048]{1,0:T(8,128)}) %reduce-scatter.2.cloned.1.call-update) | async-done | bytes 262160 | tf_op jit(solution)/shard_map/reduce_scatter | solution.py:85
  (91 shorter events, 7.2 us)
Async XLA Ops:
  8.4 19.7 %collective-permute-start = (bf16[16,3,63]{2,0,1:T(8,128)(2,1)S(1)}, bf16[16,3,63]{2,0,1:T(8,128)(2,1)S(1)}, u32[]{:S(2)}, u32[]{:S(2)}) collective-permute-start(bf16[16,3,63]{2,0,1:T(8,128)(2,1)S(1)} %slice.304), channel_id=1, source_target_pairs={{0,4},{4,8},{8,12},{1,5},{5,9},{9,13},{2,6},{6,10},{10,14},{3,7},{... | collective-permute-start | bytes 18152 | tf_op jit(solution)/shard_map/ppermute | solution.py:14
  44.5 9.2 %all-to-all-start = ((bf16[16,3,1024]{2,1,0:T(4,128)(2,1)}), bf16[16,3,1024]{2,1,0:T(4,128)(2,1)S(1)}, u32[]{:S(2)}, u32[]{:S(2)}) async-start(bf16[16,3,1024]{2,1,0:T(4,128)(2,1)} %reshape.75), calls=%async_computation | async-start | bytes 262144 | tf_op jit(solution)/shard_map/all_to_all | solution.py:67
  64.3 7.6 %all-to-all-start.1 = ((bf16[2,2,12288]{2,1,0:T(2,128)(2,1)}), bf16[2,2,12288]{2,1,0:T(2,128)(2,1)S(1)}, u32[]{:S(2)}, u32[]{:S(2)}) async-start(bf16[2,2,12288]{2,1,0:T(2,128)(2,1)} %reshape.81), calls=%async_computation.1 | async-start | bytes 196608 | tf_op jit(solution)/shard_map/all_to_all | solution.py:66
  67.6 71.9 %reduce-scatter.2.cloned.1.call-start = ((), (), s32[]{:S(2)}) async-start(), calls=%async_computation.3 | async-start | bytes 1310720 | tf_op jit(solution)/shard_map/reduce_scatter | solution.py:85
  83.0 5.5 %collective-permute-start.1 = (bf16[8,3,74]{2,0,1:T(8,128)(2,1)S(1)}, bf16[8,3,74]{2,0,1:T(8,128)(2,1)S(1)}, u32[]{:S(2)}, u32[]{:S(2)}) collective-permute-start(bf16[8,3,74]{2,0,1:T(8,128)(2,1)S(1)} %slice.305), channel_id=1, source_target_pairs={{2,0},{3,1},{6,4},{7,5},{10,8},{11,9},{14,12},{15,13},{18,16},{19,... | collective-permute-start | bytes 10664 | tf_op jit(solution)/shard_map/ppermute | solution.py:14
  96.0 3.0 %copy-start = (bf16[8,3,75,2048]{3,0,1,2:T(8,128)(2,1)}, bf16[8,3,75,2048]{3,0,1,2:T(8,128)(2,1)S(1)}, u32[]{:S(2)}) copy-start(bf16[8,3,75,2048]{3,0,1,2:T(8,128)(2,1)S(1)} %constant_dynamic-update-slice_fusion.2) | copy-start | bytes 22118404
Sparse Core Ops, SparseCore 0:
  114.0 25.4 reduce-scatter.1
where the time goes:
time: 147 us; the launch traced here: 146 us
  waiting for transfers between devices  39 us (27%)
  local copies, waits for them, and re-layouts  35.5 us (24%)
  matrix products  21.2 us (14%)
  between operations  14.1 us (10%)
  blocking collectives  13.7 us (9%)
  starting transfers between devices  13.1 us (9%)
  other arithmetic  9.66 us (7%)
    reduce_scatter x1, waiting for transfers between devices, body(): stacked = lax.psum_scatter(totals, 'corr', scatter_dimension=0, tiled=True)  25.6 us
    unnamed x79, local copies, waits for them, and re-layouts  19.2 us
    all_gather x1, blocking collectives, body(): lax.all_gather(templates, 'corr', axis=0, tiled=True)  13.7 us
    conv_general_dilated x1, matrix products, body(): lax.conv_general_dilated(extended, kernel, (DEC,), 'VALID', dimension_num...  11.7 us
    dot_general x1, matrix products, body(): partial_rows = jnp.dot(weights, scaled, preferred_element_type=jnp.float32)  9.56 us
    ppermute x2, starting transfers between devices, from_behind(): return lax.ppermute(block, axis, route)  6.42 us
    all_to_all x3, local copies, waits for them, and re-layouts, body(): lax.all_to_all(lax.all_to_all(filtered, 'corr', split_axis=0, concat_axis...  5.94 us
    all_to_all x1, waiting for transfers between devices, body(): lax.all_to_all(filtered, 'corr', split_axis=0, concat_axis=2, tiled=True)  5.86 us
  transfers between devices with their start and end apart: 5, of which 4 were waited for; matrix products, arithmetic and copies ran while one was open for 1% of the time, Pallas kernels for 0%

commit v1 on v0

--- a/solution.py
+++ b/solution.py
@@ -6,6 +6,19 @@
 L = 75
 TAPS = 64
 DEC = 4
+
+
+def _start_strings(my_data, axis_no, xx):
+    m_next, y2 = (my_data.shape[:axis_no], my_data.shape[axis_no + 1 :])
+    passed = jnp.moveaxis(my_data.reshape(*m_next, xx, -1, *y2), axis_no, 0)
+    return passed
+
+
+def fill_desk(x_local, k_dim):
+    piece_next = list(x_local.shape[1:])
+    piece_next[k_dim] *= x_local.shape[0]
+    newest = jnp.moveaxis(x_local, 0, k_dim).reshape(piece_next)
+    return newest
 
 
 def from_behind(block, axis, distance):
@@ -63,8 +76,22 @@
     )
     decimated = raw_width // DEC
     filtered = filtered.astype(jnp.bfloat16).reshape(local_stations, 3, decimated)
+
+    def bring_heads(tile_in, along_axis, state, piece_in):
+        f_now = lax.axis_size(along_axis)
+        t1 = lax.axis_index(along_axis)
+        taken_in, state_now = (f_now, t1)
+        w_next = _start_strings(tile_in, state, taken_in)
+        pages = [w_next[state_now]]
+        for dd in range(1, taken_in):
+            extra = w_next[state_now ^ dd]
+            pages.append(lax.ppermute(extra, along_axis, [(w, w ^ dd) for w in range(taken_in)]))
+        w_next = jnp.stack(pages)[state_now ^ jnp.arange(taken_in)]
+        current_value = fill_desk(w_next, piece_in)
+        return current_value
+
     moved = lax.all_to_all(
-        lax.all_to_all(filtered, "corr", split_axis=0, concat_axis=2, tiled=True),
+        bring_heads(filtered, along_axis="corr", state=0, piece_in=2),
         "filt",
         split_axis=2,
         concat_axis=0,

time: 147 us -> 145 us (0.986)
  waiting for transfers between devices: 39 us -> 36.5 us
    all_to_all x2 -> x1, waiting for transfers between devices: 9.37 us -> 3.51 us  [body(): lax.all_to_all(bring_heads(filtered, along_axis='corr', state=0, piece_in...]
    all_to_all x4 -> x3, local copies, waits for them, and re-layouts: 10.7 us -> 5.94 us  [body(): lax.all_to_all(bring_heads(filtered, along_axis='corr', state=0, piece_in...]
    reshape x1, local copies, waits for them, and re-layouts: 0.73 us -> 4.76 us  [fill_desk(): newest = jnp.moveaxis(x_local, 0, k_dim).reshape(piece_next)]
    ppermute x0 -> x3, starting transfers between devices: none -> 3.55 us  [bring_heads(): lax.ppermute(extra, along_axis, [(w, w ^ dd) for w in range(taken_in)])]
    all_to_all x2 -> x1, starting transfers between devices: 6.66 us -> 3.34 us  [body(): lax.all_to_all(bring_heads(filtered, along_axis='corr', state=0, piece_in...]
    ppermute x0 -> x3, waiting for transfers between devices: none -> 2.8 us  [bring_heads(): lax.ppermute(extra, along_axis, [(w, w ^ dd) for w in range(taken_in)])]
  transfers between devices with their start and end apart: 5 -> 7, of which waited for: 4 -> 5; matrix products, arithmetic and copies ran while one was open for 1% -> 1% of each run, Pallas kernels for 0% -> 0%
where the time goes in v1:
time: 145 us; the launch traced here: 144 us
  waiting for transfers between devices  36.5 us (25%)
  local copies, waits for them, and re-layouts  35.6 us (25%)
  matrix products  21.2 us (15%)
  between operations  14.1 us (10%)
  blocking collectives  13.7 us (9%)
  starting transfers between devices  13.3 us (9%)
  other arithmetic  9.79 us (7%)
    reduce_scatter x1, waiting for transfers between devices, body(): stacked = lax.psum_scatter(totals, 'corr', scatter_dimension=0, tiled=True)  26.2 us
    unnamed x79, local copies, waits for them, and re-layouts  19.2 us
    all_gather x1, blocking collectives, body(): lax.all_gather(templates, 'corr', axis=0, tiled=True)  13.7 us
    conv_general_dilated x1, matrix products, body(): lax.conv_general_dilated(extended, kernel, (DEC,), 'VALID', dimension_num...  11.7 us
    dot_general x1, matrix products, body(): partial_rows = jnp.dot(weights, scaled, preferred_element_type=jnp.float32)  9.56 us
    ppermute x2, starting transfers between devices, from_behind(): return lax.ppermute(block, axis, route)  6.42 us
    all_to_all x3, local copies, waits for them, and re-layouts, body(): lax.all_to_all(bring_heads(filtered, along_axis='corr', state=0, piece_in...  5.94 us
    convert_element_type x1, other arithmetic, scaled_rows(): (slices / jnp.sqrt(jnp.maximum(energy, 1.0))[:, :, None, :]).astype(jnp.b...  5.31 us
  transfers between devices with their start and end apart: 7, of which 5 were waited for; matrix products, arithmetic and copies ran while one was open for 1% of the time, Pallas kernels for 0%

profile of v1, /device:TPU:0, one launch (start us, length us, event | category | flops | bytes accessed | tf_op | source)
XLA Modules:
  0.0 144.4 jit_solution(7350421874374603610)
XLA Ops:
  6.5 0.8 broadcast_compare_fusion
  7.3 1.0 bitcast_select_fusion
  8.4 4.9 %collective-permute-start = (bf16[16,3,63]{2,0,1:T(8,128)(2,1)S(1)}, bf16[16,3,63]{2,0,1:T(8,128)(2,1)S(1)}, u32[]{:S(2)}, u32[]{:S(2)}) collective-permute-start(bf16[16,3,63]{2,0,1:T(8,128)(2,1)S(1)} %slice.306), channel_id=1, source_target_pairs={{0,4},{4,8},{8,12},{1,5},{5,9},{9,13},{2,6},{6,10},{10,14},{3,7},{... | collective-permute-start | bytes 18152 | tf_op jit(solution)/shard_map/ppermute | solution.py:27
  13.4 13.7 %all_gather.3 = bf16[128,225]{1,0:T(8,128)(2,1)S(1)} all-gather(bf16[32,225]{1,0:T(8,128)(2,1)} %param.8), channel_id=1, replica_groups=mesh['groups'=2,'corr'=4,'filt'=2,'pair'=2] {'corr'}, dimensions={0}, use_global_device_ids=true | all-gather | bytes 72000 | tf_op jit(solution)/shard_map/all_gather | solution.py:109
  27.3 0.7 rev.3
  28.1 0.1 copy.133
  28.2 0.2 pad_maximum_fusion
  28.4 0.2 copy.131
  28.6 0.3 reshape.89
  29.0 2.8 %copy.132 = bf16[48,1,4159]{0,1,2:T(2,128)(2,1)S(1)} copy(bf16[48,1,4159]{2,0,1:T(8,128)(2,1)S(1)} %reshape.89) | data formatting | bytes 798528 | tf_op jit(solution)/shard_map/reshape | solution.py:65
  31.8 11.7 %convolution_convert_fusion = bf16[48,1,1024]{0,1,2:T(2,128)(2,1)S(1)} fusion(bf16[48,1,4159]{0,1,2:T(2,128)(2,1)S(1)} %copy.132, bf16[1,1,64]{1,0,2:T(2,128)(2,1)S(1)} %copy.133), kind=kOutput, calls=%fused_computation.7 | convolution fusion | flops 6340608 | bytes 497696 | tf_op jit(solution)/shard_map/conv_general_dilated | solution.py:69
  43.5 0.3 copy.134
  44.0 0.6 collective-permute-start.2
  44.6 1.2 collective-permute-start.3
  45.8 1.7 %collective-permute-start.1 = (bf16[4,3,1024]{2,1,0:T(4,128)(2,1)S(1)}, bf16[4,3,1024]{2,1,0:T(4,128)(2,1)S(1)}, u32[]{:S(2)}, u32[]{:S(2)}) collective-permute-start(bf16[4,3,1024]{2,1,0:T(4,128)(2,1)S(1)} %get-tuple-element.8), channel_id=1, source_target_pairs={{0,4},{4,0},{8,12},{12,8},{1,5},{5,1},{9,13},{13,9},{2,6},{6,2},{1... | collective-permute-start | bytes 73736 | tf_op jit(solution)/shard_map/ppermute | solution.py:88
  47.5 1.3 collective-permute-done.2
  48.8 1.5 %collective-permute-done.3 = bf16[4,3,1024]{2,1,0:T(4,128)(2,1)S(1)} collective-permute-done((bf16[4,3,1024]{2,1,0:T(4,128)(2,1)S(1)}, bf16[4,3,1024]{2,1,0:T(4,128)(2,1)S(1)}, u32[]{:S(2)}, u32[]{:S(2)}) %collective-permute-start.3) | collective-permute-done | bytes 24608 | tf_op jit(solution)/shard_map/ppermute | solution.py:88
  50.4 0.7 gather_fusion
  51.1 4.8 %copy.148 = bf16[4,3,4,1024]{0,1,3,2:T(4,128)(2,1)} copy(bf16[4,3,4,1024]{3,1,0,2:T(4,128)(2,1)S(1)} %bitcast.344) | data formatting | bytes 196608 | tf_op jit(solution)/shard_map/reshape | solution.py:20
  55.9 5.8 %reshape.105 = bf16[2,2,12288]{2,1,0:T(2,128)(2,1)} reshape(bf16[4096,3,4]{2,1,0:T(4,128)(2,1)} %bitcast.342) | data formatting | bytes 196608
  61.7 3.3 %all-to-all-start = ((bf16[2,2,12288]{2,1,0:T(2,128)(2,1)}), bf16[2,2,12288]{2,1,0:T(2,128)(2,1)S(1)}, u32[]{:S(2)}, u32[]{:S(2)}) async-start(bf16[2,2,12288]{2,1,0:T(2,128)(2,1)} %reshape.105), calls=%async_computation | async-start | bytes 196608 | tf_op jit(solution)/shard_map/all_to_all | solution.py:93
  65.1 0.7 dynamic-slice_convert_fusion
  65.8 3.5 %all-to-all-done = bf16[2,2,12288]{2,1,0:T(2,128)(2,1)S(1)} async-done(((bf16[2,2,12288]{2,1,0:T(2,128)(2,1)}), bf16[2,2,12288]{2,1,0:T(2,128)(2,1)S(1)}, u32[]{:S(2)}, u32[]{:S(2)}) %all-to-all-start) | async-done | bytes 98336 | tf_op jit(solution)/shard_map/all_to_all | solution.py:93
  69.3 5.1 %reshape.106 = bf16[4096,3,4]{2,1,0:T(4,128)(2,1)} reshape(bf16[2,2,12288]{2,1,0:T(2,128)(2,1)S(1)} %all-to-all-done) | data formatting | bytes 196608
  74.4 5.9 %copy.149 = bf16[4,3,2,2048]{3,2,0,1:T(2,128)(2,1)S(1)} copy(bf16[4,3,2,2048]{0,1,3,2:T(4,128)(2,1)} %bitcast.343) | data formatting | bytes 196608 | tf_op jit(solution)/shard_map/all_to_all | solution.py:93
  80.4 1.5 %collective-permute-start.4 = (bf16[8,3,74]{2,0,1:T(8,128)(2,1)S(1)}, bf16[8,3,74]{2,0,1:T(8,128)(2,1)S(1)}, u32[]{:S(2)}, u32[]{:S(2)}) collective-permute-start(bf16[8,3,74]{2,0,1:T(8,128)(2,1)S(1)} %slice.307), channel_id=1, source_target_pairs={{2,0},{3,1},{6,4},{7,5},{10,8},{11,9},{14,12},{15,13},{18,16},{19,... | collective-permute-start | bytes 10664 | tf_op jit(solution)/shard_map/ppermute | solution.py:27
  81.9 4.0 %collective-permute-done.4 = bf16[8,3,74]{2,0,1:T(8,128)(2,1)S(1)} collective-permute-done((bf16[8,3,74]{2,0,1:T(8,128)(2,1)S(1)}, bf16[8,3,74]{2,0,1:T(8,128)(2,1)S(1)}, u32[]{:S(2)}, u32[]{:S(2)}) %collective-permute-start.4) | collective-permute-done | bytes 3584 | tf_op jit(solution)/shard_map/ppermute | solution.py:27
  93.5 1.6 %fusion = f32[8,3,2048]{2,0,1:T(8,128)S(1)} fusion(bf16[8,3,75,2048]{3,0,1,2:T(8,128)(2,1)S(1)} %constant_dynamic-update-slice_fusion.2), kind=kLoop, calls=%fused_computation.2 | loop fusion | flops 11010048 | bytes 7569408 | tf_op jit(solution)/shard_map/scjt,scjt->sct/dot_general | solution.py:34
  95.0 1.4 copy-done
  96.5 5.3 %divide_convert_fusion = bf16[8,3,75,2048]{3,0,1,2:T(8,128)(2,1)S(1)} fusion(bf16[8,3,75,2048]{3,0,1,2:T(8,128)(2,1)} %copy-done, f32[8,3,2048]{2,0,1:T(8,128)S(1)} %maximum_sqrt_fusion), kind=kLoop, calls=%fused_computation.3 | loop fusion | flops 11059200 | bytes 14942208 | tf_op jit(solution)/shard_map/convert_element_type | solution.py:35
  101.8 9.6 %fusion.3 = f32[128,2048]{1,0:T(8,128)} fusion(bf16[8,3,75,2048]{3,0,1,2:T(8,128)(2,1)S(1)} %divide_convert_fusion, f32[128,8,3]{0,2,1:T(4,128)S(1)} %bitcast.346, f32[128,3,75]{0,2,1:T(8,128)S(1)} %broadcast_divide_fusion), kind=kOutput, calls=%fused_computation.6 | convolution fusion | flops 944179200 | bytes 8548864 | tf_op jit(solution)/shard_map/dot_general | solution.py:110
  111.4 26.2 %reduce-scatter.2.cloned.1.call-done = f32[32,2048]{1,0:T(8,128)} async-done(((f32[128,2048]{1,0:T(8,128)}), f32[32,2048]{1,0:T(8,128)}) %reduce-scatter.2.cloned.1.call-update) | async-done | bytes 262160 | tf_op jit(solution)/shard_map/reduce_scatter | solution.py:112
  (100 shorter events, 7.8 us)
Async XLA Ops:
  8.4 19.8 %collective-permute-start = (bf16[16,3,63]{2,0,1:T(8,128)(2,1)S(1)}, bf16[16,3,63]{2,0,1:T(8,128)(2,1)S(1)}, u32[]{:S(2)}, u32[]{:S(2)}) collective-permute-start(bf16[16,3,63]{2,0,1:T(8,128)(2,1)S(1)} %slice.306), channel_id=1, source_target_pairs={{0,4},{4,8},{8,12},{1,5},{5,9},{9,13},{2,6},{6,10},{10,14},{3,7},{... | collective-permute-start | bytes 18152 | tf_op jit(solution)/shard_map/ppermute | solution.py:27
  44.0 4.9 %collective-permute-start.2 = (bf16[4,3,1024]{2,1,0:T(4,128)(2,1)S(1)}, bf16[4,3,1024]{2,1,0:T(4,128)(2,1)S(1)}, u32[]{:S(2)}, u32[]{:S(2)}) collective-permute-start(bf16[4,3,1024]{2,1,0:T(4,128)(2,1)S(1)} %get-tuple-element.7), channel_id=1, source_target_pairs={{0,8},{4,12},{8,0},{12,4},{1,9},{5,13},{9,1},{13,5},{2,10},{6,14},... | collective-permute-start | bytes 73736 | tf_op jit(solution)/shard_map/ppermute | solution.py:88
  44.6 5.7 %collective-permute-start.3 = (bf16[4,3,1024]{2,1,0:T(4,128)(2,1)S(1)}, bf16[4,3,1024]{2,1,0:T(4,128)(2,1)S(1)}, u32[]{:S(2)}, u32[]{:S(2)}) collective-permute-start(bf16[4,3,1024]{2,1,0:T(4,128)(2,1)S(1)} %get-tuple-element.6), channel_id=1, source_target_pairs={{0,12},{4,8},{8,4},{12,0},{1,13},{5,9},{9,5},{13,1},{2,14},{6,10},... | collective-permute-start | bytes 73736 | tf_op jit(solution)/shard_map/ppermute | solution.py:88
  45.8 4.5 %collective-permute-start.1 = (bf16[4,3,1024]{2,1,0:T(4,128)(2,1)S(1)}, bf16[4,3,1024]{2,1,0:T(4,128)(2,1)S(1)}, u32[]{:S(2)}, u32[]{:S(2)}) collective-permute-start(bf16[4,3,1024]{2,1,0:T(4,128)(2,1)S(1)} %get-tuple-element.8), channel_id=1, source_target_pairs={{0,4},{4,0},{8,12},{12,8},{1,5},{5,1},{9,13},{13,9},{2,6},{6,2},{1... | collective-permute-start | bytes 73736 | tf_op jit(solution)/shard_map/ppermute | solution.py:88
  61.7 7.6 %all-to-all-start = ((bf16[2,2,12288]{2,1,0:T(2,128)(2,1)}), bf16[2,2,12288]{2,1,0:T(2,128)(2,1)S(1)}, u32[]{:S(2)}, u32[]{:S(2)}) async-start(bf16[2,2,12288]{2,1,0:T(2,128)(2,1)} %reshape.105), calls=%async_computation | async-start | bytes 196608 | tf_op jit(solution)/shard_map/all_to_all | solution.py:93
  65.1 72.5 %reduce-scatter.2.cloned.1.call-start = ((), (), s32[]{:S(2)}) async-start(), calls=%async_computation.2 | async-start | bytes 1310720 | tf_op jit(solution)/shard_map/reduce_scatter | solution.py:112
  80.4 5.5 %collective-permute-start.4 = (bf16[8,3,74]{2,0,1:T(8,128)(2,1)S(1)}, bf16[8,3,74]{2,0,1:T(8,128)(2,1)S(1)}, u32[]{:S(2)}, u32[]{:S(2)}) collective-permute-start(bf16[8,3,74]{2,0,1:T(8,128)(2,1)S(1)} %slice.307), channel_id=1, source_target_pairs={{2,0},{3,1},{6,4},{7,5},{10,8},{11,9},{14,12},{15,13},{18,16},{19,... | collective-permute-start | bytes 10664 | tf_op jit(solution)/shard_map/ppermute | solution.py:27
  93.4 3.0 %copy-start = (bf16[8,3,75,2048]{3,0,1,2:T(8,128)(2,1)}, bf16[8,3,75,2048]{3,0,1,2:T(8,128)(2,1)S(1)}, u32[]{:S(2)}) copy-start(bf16[8,3,75,2048]{3,0,1,2:T(8,128)(2,1)S(1)} %constant_dynamic-update-slice_fusion.2) | copy-start | bytes 22118404
Sparse Core Ops, SparseCore 0:
  111.5 26.0 reduce-scatter.1
